TPU v7x, 32 devices: a whole 2x2x4 slice. The times are simulated.
32 devices in a mesh: dp: 2 (over y), seq: 16 (over z, x, core).
Axes of the slice: x: 2, y: 2, z: 4, core: 2. Of those that a mesh axis runs over, the one named last changes fastest.
Arguments:
- inputs: bfloat16 [2, 256, 512, 512], P('dp', 'seq'), may hold values from -6 to 6
- gate_logits: bfloat16 [2, 256, 512, 512], P('dp', 'seq'), may hold values from -8 to 8
- kernel: bfloat16 [256, 512, 512], P(None, 'seq'), may hold values from -1.5 to 1.5
- cotangent: bfloat16 [2, 256, 512, 512], P('dp', 'seq'), may hold values from -6 to 6
- block_one: bfloat16 [256, 512, 512], P('seq'), may hold values from -0.25 to 0.25
- block_two: bfloat16 [512, 256, 256], P('seq'), may hold values from -0.375 to 0.375
Outputs:
- output: bfloat16 [2, 256, 512, 512], P('dp', 'seq')
- grad_inputs: bfloat16 [2, 256, 512, 512], P('dp', 'seq')
- grad_gate: bfloat16 [2, 256, 512, 512], P('dp', 'seq')
- grad_kernel: bfloat16 [256, 512, 512], P(None, 'seq', 'dp')
- grad_block_one: bfloat16 [256, 512, 512], P('seq', None, 'dp')
- grad_block_two: bfloat16 [512, 256, 256], P('seq', None, 'dp')
All inputs are finite; a program needn't handle non-finite values.
Results may differ from a plain program's by a relative error of at most 0.009.
Values may be sent and summed in bfloat16 or wider, within the bound.
No kernel may reach another device: no remote copies, remote signals or barrier semaphores. Data moves between devices by JAX's collectives and lax.ppermute only.
A program may use at most 320 MiB of HBM per device.

v0:
```python
import jax
import jax.numpy as jnp
from jax import lax
from jax.sharding import PartitionSpec as P


def body(inputs, gate_logits, kernel, cotangent, block_one, block_two):
    tokens = inputs[0]
    kernel_wide = kernel.astype(jnp.float32)
    grad_scale = (lax.axis_size("dp") * tokens.shape[2]) ** (-0.5)
    first = jnp.einsum(
        "acb,abd->acd", block_one, tokens, preferred_element_type=jnp.float32
    ).astype(jnp.bfloat16)
    arrived = lax.all_to_all(first, "seq", split_axis=1, concat_axis=0, tiled=True)
    first_cols = arrived
    second = jnp.einsum("cea,acd->ecd", block_two, arrived, preferred_element_type=jnp.float32)
    filtered = (kernel_wide * second).astype(jnp.bfloat16)
    third = jnp.einsum(
        "cef,ecd->fcd", block_two, filtered, preferred_element_type=jnp.float32
    ).astype(jnp.bfloat16)
    arrived = lax.all_to_all(third, "seq", split_axis=0, concat_axis=1, tiled=True)
    third_rows = arrived
    fourth = jnp.einsum(
        "fch,fcd->fhd", block_one, arrived, preferred_element_type=jnp.float32
    ).astype(jnp.bfloat16)
    opened = jax.nn.sigmoid(gate_logits[0].astype(jnp.float32))
    incoming = cotangent[0].astype(jnp.float32)
    fourth_wide = fourth.astype(jnp.float32)
    output = (opened * fourth_wide).astype(jnp.bfloat16)
    grad_gate = (incoming * fourth_wide * opened * (1.0 - opened)).astype(jnp.bfloat16)
    grad_fourth = (incoming * opened).astype(jnp.bfloat16)
    outer_one = jnp.einsum(
        "fhd,fcd->fch", grad_fourth, third_rows, preferred_element_type=jnp.float32
    )
    grad_third = jnp.einsum(
        "fch,fhd->fcd", block_one, grad_fourth, preferred_element_type=jnp.float32
    ).astype(jnp.bfloat16)
    arrived = lax.all_to_all(grad_third, "seq", split_axis=1, concat_axis=0, tiled=True)
    grad_third_cols = arrived
    grad_filtered = jnp.einsum(
        "cef,fcd->ecd", block_two, arrived, preferred_element_type=jnp.float32
    )
    outer_two = jnp.einsum(
        "fcd,ecd->cef", grad_third_cols, filtered, preferred_element_type=jnp.float32
    )
    grad_kernel = grad_filtered * second
    grad_second = (kernel_wide * grad_filtered).astype(jnp.bfloat16)
    grad_block_two = (
        outer_two
        + jnp.einsum("ecd,acd->cea", grad_second, first_cols, preferred_element_type=jnp.float32)
    ) * grad_scale
    grad_first = jnp.einsum(
        "cea,ecd->acd", block_two, grad_second, preferred_element_type=jnp.float32
    ).astype(jnp.bfloat16)
    arrived = lax.all_to_all(grad_first, "seq", split_axis=0, concat_axis=1, tiled=True)
    grad_tokens = jnp.einsum(
        "acb,acd->abd", block_one, arrived, preferred_element_type=jnp.float32
    ).astype(jnp.bfloat16)
    grad_block_one = (
        outer_one + jnp.einsum("acd,abd->acb", arrived, tokens, preferred_element_type=jnp.float32)
    ) * grad_scale
    grad_block_one, grad_block_two, grad_kernel = (
        lax.psum_scatter(grad_block_one, "dp", scatter_dimension=2, tiled=True),
        lax.psum_scatter(grad_block_two, "dp", scatter_dimension=2, tiled=True),
        lax.psum_scatter(grad_kernel, "dp", scatter_dimension=2, tiled=True),
    )
    return (
        output[None],
        grad_tokens[None],
        grad_gate[None],
        grad_kernel.astype(jnp.bfloat16),
        grad_block_one.astype(jnp.bfloat16),
        grad_block_two.astype(jnp.bfloat16),
    )


def solution(mesh):
    return jax.shard_map(
        body,
        mesh=mesh,
        in_specs=(
            P("dp", "seq", None, None),
            P("dp", "seq", None, None),
            P(None, "seq", None),
            P("dp", "seq", None, None),
            P("seq", None, None),
            P("seq", None, None),
        ),
        out_specs=(
            P("dp", "seq", None, None),
            P("dp", "seq", None, None),
            P("dp", "seq", None, None),
            P(None, "seq", "dp"),
            P("seq", None, "dp"),
            P("seq", None, "dp"),
        ),
        check_vma=False,
    )
```

profile of v0, /device:TPU:0, one launch (start us, length us, event | category | flops | bytes accessed | tf_op | source)
XLA Modules:
  0.0 1188.4 jit_solution(1900922170163310603)
XLA Ops:
  7.2 12.3 %copy.77 = bf16[1,16,512,512]{2,3,1,0:T(8,128)(2,1)} copy(bf16[1,16,512,512]{3,2,1,0:T(8,128)(2,1)} %param.7) | data formatting | bytes 16777216 | tf_op args[1]
  19.4 12.3 %copy.86 = bf16[1,16,512,512]{2,3,1,0:T(8,128)(2,1)} copy(bf16[1,16,512,512]{3,2,1,0:T(8,128)(2,1)} %param.9) | data formatting | bytes 16777216 | tf_op args[3]
  31.7 12.7 %convert_bitcast_fusion.2 = bf16[16,512,512]{1,2,0:T(8,128)(2,1)} fusion(bf16[16,512,512]{2,1,0:T(8,128)(2,1)} %param.10, bf16[1,16,512,512]{2,3,1,0:T(8,128)(2,1)} %copy.86, bf16[1,16,512,512]{2,3,1,0:T(8,128)(2,1)} %copy.77), kind=kOutput, calls=%fused_computation.25 | convolution fusion | flops 4328521728 | bytes 33554432 | tf_op jit(solution)/shard_map/fch,fhd->fcd/dot_general | solution.py:35
  44.4 14.9 %copy.87 = bf16[16,512,512]{2,0,1:T(8,128)(2,1)} copy(bf16[16,512,512]{1,2,0:T(8,128)(2,1)} %convert_bitcast_fusion.2) | data formatting | bytes 16777216 | tf_op jit(solution)/shard_map/convert_element_type | solution.py:37
  59.3 7.6 all-to-all-start.2
  66.9 13.7 %fusion.21 = bf16[16,512,512]{2,1,0:T(8,128)(2,1)} fusion(bf16[16,512,512]{2,1,0:T(8,128)(2,1)} %param.10, bf16[1,16,512,512]{3,2,1,0:T(8,128)(2,1)} %param.6), kind=kOutput, calls=%fused_computation.35 | convolution fusion | flops 4299161600 | bytes 25165824 | tf_op jit(solution)/shard_map/acb,abd->acd/dot_general | solution.py:11
  80.6 11.3 copy.79
  91.9 125.5 %all-to-all-done.2 = bf16[16,512,512]{2,0,1:T(8,128)(2,1)} async-done(((bf16[16,512,512]{2,0,1:T(8,128)(2,1)}), bf16[16,512,512]{2,0,1:T(8,128)(2,1)}, u32[]{:S(2)}, u32[]{:S(2)}) %all-to-all-start.2) | async-done | bytes 8388640 | tf_op jit(solution)/shard_map/all_to_all | solution.py:38
  217.5 36.5 %all-to-all-start = ((bf16[16,512,512]{2,0,1:T(8,128)(2,1)}), bf16[16,512,512]{2,0,1:T(8,128)(2,1)}, u32[]{:S(2)}, u32[]{:S(2)}) async-start(bf16[16,512,512]{2,0,1:T(8,128)(2,1)} %copy.79), calls=%async_computation | async-start | bytes 16777216 | tf_op jit(solution)/shard_map/all_to_all | solution.py:14
  254.0 0.0 reduce-scatter.8.cloned.1.call-start
  254.0 13.9 %copy.78 = bf16[256,32,512]{0,2,1:T(8,128)(2,1)} copy(bf16[256,32,512]{2,1,0:T(8,128)(2,1)} %param.8) | data formatting | bytes 16777216 | tf_op args[2]
  267.9 12.3 %copy.89 = bf16[16,16,32,512]{3,2,1,0:T(8,128)(2,1)} copy(bf16[16,16,32,512]{3,1,2,0:T(8,128)(2,1)} %bitcast.17) | data formatting | bytes 16777216 | tf_op jit(solution)/shard_map/all_to_all | solution.py:38
  280.2 124.3 %all-to-all-done = bf16[16,512,512]{2,0,1:T(8,128)(2,1)} async-done(((bf16[16,512,512]{2,0,1:T(8,128)(2,1)}), bf16[16,512,512]{2,0,1:T(8,128)(2,1)}, u32[]{:S(2)}, u32[]{:S(2)}) %all-to-all-start) | async-done | bytes 8388640 | tf_op jit(solution)/shard_map/all_to_all | solution.py:14
  404.6 12.7 %copy.81 = bf16[16,16,32,512]{3,2,1,0:T(8,128)(2,1)} copy(bf16[16,16,32,512]{3,1,2,0:T(8,128)(2,1)} %bitcast.4) | data formatting | bytes 16777216 | tf_op jit(solution)/shard_map/all_to_all | solution.py:14
  417.3 20.4 %fusion.13 = f32[32,512,256]{2,1,0:T(8,128)} fusion(bf16[32,256,256]{2,1,0:T(8,128)(2,1)} %param.11, bf16[256,32,512]{2,1,0:T(8,128)(2,1)} %bitcast.89), kind=kOutput, calls=%fused_computation.27 | convolution fusion | flops 2147483648 | bytes 29360128 | tf_op jit(solution)/shard_map/cea,acd->ecd/dot_general | solution.py:16
  437.6 22.1 %bitcast_multiply_fusion = (f32[256,32,512]{0,2,1:T(8,128)}, f32[32,512,256]{2,1,0:T(8,128)}) fusion(f32[32,512,256]{2,1,0:T(8,128)} %fusion.13, bf16[32,256,256]{2,1,0:T(8,128)(2,1)} %param.11, bf16[256,32,512]{2,1,0:T(8,128)(2,1)} %bitcast.87), kind=kOutput, calls=%fused_computation.10 | convolution fusion | flops 2151677952 | bytes 62914560 | tf_op jit(solution)/shard_map/cef,fcd->ecd/dot_general | solution.py:40
  459.7 21.2 %fusion.15 = f32[32,256,256]{2,1,0:T(8,128)} fusion(bf16[256,32,512]{2,1,0:T(8,128)(2,1)} %bitcast.90, bf16[256,32,512]{0,2,1:T(8,128)(2,1)} %copy.78, f32[32,512,256]{2,1,0:T(8,128)} %get-tuple-element.33), kind=kOutput, calls=%fused_computation.29 | convolution fusion | flops 2160066560 | bytes 41943040 | tf_op jit(solution)/shard_map/ecd,acd->cea/dot_general | solution.py:50
  481.0 23.3 %add_multiply_fusion.1 = f32[32,256,256]{2,1,0:T(8,128)} fusion(f32[32,256,256]{2,1,0:T(8,128)} %fusion.15, bf16[256,32,512]{2,1,0:T(8,128)(2,1)} %bitcast.88, bf16[256,32,512]{0,2,1:T(8,128)(2,1)} %copy.78, f32[32,512,256]{2,1,0:T(8,128)} %fusion.13), kind=kOutput, calls=%fused_computation.22 | convolution fusion | flops 2164260864 | bytes 50331648 | tf_op jit(solution)/shard_map/fcd,ecd->cef/dot_general | solution.py:43
  504.3 0.0 reduce-scatter.8.cloned.1.call-update
  504.3 14.2 %convert_bitcast_fusion.3 = bf16[256,32,512]{0,2,1:T(8,128)(2,1)} fusion(bf16[32,256,256]{2,1,0:T(8,128)(2,1)} %param.11, bf16[256,32,512]{0,2,1:T(8,128)(2,1)} %copy.78, f32[32,512,256]{2,1,0:T(8,128)} %fusion.13), kind=kOutput, calls=%fused_computation.26 | convolution fusion | flops 2164260864 | bytes 37748736 | tf_op jit(solution)/shard_map/cef,ecd->fcd/dot_general | solution.py:18
  518.5 14.6 %copy.83 = bf16[256,32,512]{2,1,0:T(8,128)(2,1)} copy(bf16[256,32,512]{0,2,1:T(8,128)(2,1)} %convert_bitcast_fusion.3) | data formatting | bytes 16777216 | tf_op jit(solution)/shard_map/convert_element_type | solution.py:20
  533.2 37.2 %all-to-all-start.1 = ((bf16[256,32,512]{2,1,0:T(8,128)(2,1)}), bf16[256,32,512]{2,1,0:T(8,128)(2,1)}, u32[]{:S(2)}, u32[]{:S(2)}) async-start(bf16[256,32,512]{2,1,0:T(8,128)(2,1)} %copy.83), calls=%async_computation.1 | async-start | bytes 16777216 | tf_op jit(solution)/shard_map/all_to_all | solution.py:21
  570.4 0.0 reduce-scatter.4.cloned.1.call-start
  570.4 0.7 reduce-scatter.4.cloned.1.call-update
  571.1 14.6 %convert_bitcast_fusion.1 = bf16[256,32,512]{0,2,1:T(8,128)(2,1)} fusion(bf16[32,256,256]{2,1,0:T(8,128)(2,1)} %param.11, bf16[256,32,512]{0,2,1:T(8,128)(2,1)} %copy.78, f32[32,512,256]{2,1,0:T(8,128)} %get-tuple-element.33), kind=kOutput, calls=%fused_computation.24 | convolution fusion | flops 2164260864 | bytes 37748736 | tf_op jit(solution)/shard_map/cea,ecd->acd/dot_general | solution.py:52
  585.7 14.8 %copy.91 = bf16[256,32,512]{2,1,0:T(8,128)(2,1)} copy(bf16[256,32,512]{0,2,1:T(8,128)(2,1)} %convert_bitcast_fusion.1) | data formatting | bytes 16777216 | tf_op jit(solution)/shard_map/convert_element_type | solution.py:54
  600.5 120.5 %all-to-all-done.1 = bf16[256,32,512]{2,1,0:T(8,128)(2,1)} async-done(((bf16[256,32,512]{2,1,0:T(8,128)(2,1)}), bf16[256,32,512]{2,1,0:T(8,128)(2,1)}, u32[]{:S(2)}, u32[]{:S(2)}) %all-to-all-start.1) | async-done | bytes 8388640 | tf_op jit(solution)/shard_map/all_to_all | solution.py:21
  721.0 36.5 %all-to-all-start.3 = ((bf16[256,32,512]{2,1,0:T(8,128)(2,1)}), bf16[256,32,512]{2,1,0:T(8,128)(2,1)}, u32[]{:S(2)}, u32[]{:S(2)}) async-start(bf16[256,32,512]{2,1,0:T(8,128)(2,1)} %copy.91), calls=%async_computation.3 | async-start | bytes 16777216 | tf_op jit(solution)/shard_map/all_to_all | solution.py:55
  757.5 0.0 reduce-scatter.6.cloned.1.call-start
  757.6 8.7 copy.84
  766.2 141.8 %all-to-all-done.3 = bf16[256,32,512]{2,1,0:T(8,128)(2,1)} async-done(((bf16[256,32,512]{2,1,0:T(8,128)(2,1)}), bf16[256,32,512]{2,1,0:T(8,128)(2,1)}, u32[]{:S(2)}, u32[]{:S(2)}) %all-to-all-start.3) | async-done | bytes 8388640 | tf_op jit(solution)/shard_map/all_to_all | solution.py:55
  908.1 8.2 copy.92
  916.3 16.1 %fusion.9 = f32[16,512,512]{2,1,0:T(8,128)} fusion(bf16[16,512,512]{2,1,0:T(8,128)(2,1)} %bitcast.91, bf16[1,16,512,512]{3,2,1,0:T(8,128)(2,1)} %param.6), kind=kOutput, calls=%fused_computation.18 | convolution fusion | flops 4294967296 | bytes 33554432 | tf_op jit(solution)/shard_map/acd,abd->acb/dot_general | solution.py:60
  932.4 22.1 %add_multiply_fusion = f32[16,512,512]{2,1,0:T(8,128)} fusion(f32[16,512,512]{2,1,0:T(8,128)} %fusion.9, bf16[16,512,512]{2,1,0:T(8,128)(2,1)} %bitcast.93, bf16[1,16,512,512]{2,3,1,0:T(8,128)(2,1)} %copy.86, bf16[1,16,512,512]{2,3,1,0:T(8,128)(2,1)} %copy.77), kind=kOutput, calls=%fused_computation.14 | convolution fusion | flops 4332716032 | bytes 58720256 | tf_op jit(solution)/shard_map/fhd,fcd->fch/dot_general | solution.py:32
  954.5 0.0 reduce-scatter.6.cloned.1.call-update
  954.5 20.4 %fusion.8 = (bf16[1,16,512,512]{2,3,1,0:T(8,128)(2,1)}, bf16[1,16,512,512]{2,3,1,0:T(8,128)(2,1)}) fusion(bf16[1,16,512,512]{2,3,1,0:T(8,128)(2,1)} %copy.86, bf16[1,16,512,512]{2,3,1,0:T(8,128)(2,1)} %copy.77, bf16[16,512,512]{2,1,0:T(8,128)(2,1)} %bitcast.94, bf16[16,512,512]{2,1,0:T(8,128)(2,1)} %param.10), kind=kOutput, calls=%fused_computation.17 | convolution fusion | flops 4353687552 | bytes 50331648 | tf_op jit(solution)/shard_map/fch,fcd->fhd/dot_general | solution.py:23
  974.9 12.3 %copy.101 = bf16[1,16,512,512]{3,2,1,0:T(8,128)(2,1)} copy(bf16[1,16,512,512]{2,3,1,0:T(8,128)(2,1)} %get-tuple-element.30) | data formatting | bytes 16777216
  987.2 12.1 %copy.99 = bf16[1,16,512,512]{3,2,1,0:T(8,128)(2,1)} copy(bf16[1,16,512,512]{2,3,1,0:T(8,128)(2,1)} %get-tuple-element.31) | data formatting | bytes 16777216
  999.3 11.7 convert_bitcast_fusion
  1011.0 12.3 %copy.100 = bf16[1,16,512,512]{3,2,1,0:T(8,128)(2,1)} copy(bf16[1,16,512,512]{2,3,1,0:T(8,128)(2,1)} %convert_bitcast_fusion) | data formatting | bytes 16777216
  1023.3 0.0 reduce-scatter.8.cloned.1.call-done
  1023.3 4.1 convert_element_type.97
  1027.4 0.0 reduce-scatter.4.cloned.1.call-done
  1027.4 6.2 convert_element_type.95
  1033.6 7.8 copy.102
  1041.4 134.3 %reduce-scatter.6.cloned.1.call-done = f32[16,512,256]{2,1,0:T(8,128)} async-done(((f32[16,512,512]{2,1,0:T(8,128)}), f32[16,512,256]{2,1,0:T(8,128)}) %reduce-scatter.6.cloned.1.call-update) | async-done | bytes 8388624 | tf_op jit(solution)/shard_map/reduce_scatter | solution.py:63
  1175.7 5.9 convert_element_type.96
Async XLA Ops:
  59.3 158.2 %all-to-all-start.2 = ((bf16[16,512,512]{2,0,1:T(8,128)(2,1)}), bf16[16,512,512]{2,0,1:T(8,128)(2,1)}, u32[]{:S(2)}, u32[]{:S(2)}) async-start(bf16[16,512,512]{2,0,1:T(8,128)(2,1)} %copy.87), calls=%async_computation.2 | async-start | bytes 16777216 | tf_op jit(solution)/shard_map/all_to_all | solution.py:38
  217.5 187.1 %all-to-all-start = ((bf16[16,512,512]{2,0,1:T(8,128)(2,1)}), bf16[16,512,512]{2,0,1:T(8,128)(2,1)}, u32[]{:S(2)}, u32[]{:S(2)}) async-start(bf16[16,512,512]{2,0,1:T(8,128)(2,1)} %copy.79), calls=%async_computation | async-start | bytes 16777216 | tf_op jit(solution)/shard_map/all_to_all | solution.py:14
  254.0 769.3 %reduce-scatter.8.cloned.1.call-start = ((), (), s32[]{:S(2)}) async-start(), calls=%async_computation.9 | async-start | bytes 12582912 | tf_op jit(solution)/shard_map/reduce_scatter | solution.py:64
  533.2 187.8 %all-to-all-start.1 = ((bf16[256,32,512]{2,1,0:T(8,128)(2,1)}), bf16[256,32,512]{2,1,0:T(8,128)(2,1)}, u32[]{:S(2)}, u32[]{:S(2)}) async-start(bf16[256,32,512]{2,1,0:T(8,128)(2,1)} %copy.83), calls=%async_computation.1 | async-start | bytes 16777216 | tf_op jit(solution)/shard_map/all_to_all | solution.py:21
  570.4 457.0 %reduce-scatter.4.cloned.1.call-start = ((), (), s32[]{:S(2)}) async-start(), calls=%async_computation.7 | async-start | bytes 25165824 | tf_op jit(solution)/shard_map/reduce_scatter | solution.py:65
  721.0 187.1 %all-to-all-start.3 = ((bf16[256,32,512]{2,1,0:T(8,128)(2,1)}), bf16[256,32,512]{2,1,0:T(8,128)(2,1)}, u32[]{:S(2)}, u32[]{:S(2)}) async-start(bf16[256,32,512]{2,1,0:T(8,128)(2,1)} %copy.91), calls=%async_computation.3 | async-start | bytes 16777216 | tf_op jit(solution)/shard_map/all_to_all | solution.py:55
  757.5 418.2 %reduce-scatter.6.cloned.1.call-start = ((), (), s32[]{:S(2)}) async-start(), calls=%async_computation.8 | async-start | bytes 25165824 | tf_op jit(solution)/shard_map/reduce_scatter | solution.py:63
Sparse Core Ops, SparseCore 0:
  504.4 131.1 reduce-scatter.7
  637.9 189.1 reduce-scatter.3
  954.6 221.0 reduce-scatter.5
where the time goes:
time: 1200 us; the launch traced here: 1190 us
  waiting for transfers between devices  647 us (54%)
  matrix products  212 us (18%)
  local copies, waits for them, and re-layouts  181 us (15%)
  starting transfers between devices  118 us (10%)
  other arithmetic  16.2 us (1%)
  between operations  14.1 us (1%)
    all_to_all x1, waiting for transfers between devices, body(): lax.all_to_all(grad_first, 'seq', split_axis=0, concat_axis=1, tiled=True)  142 us
    reduce_scatter x1, waiting for transfers between devices, body(): lax.psum_scatter(grad_block_one, 'dp', scatter_dimension=2, tiled=True)  134 us
    all_to_all x1, waiting for transfers between devices, body(): lax.all_to_all(grad_third, 'seq', split_axis=1, concat_axis=0, tiled=True)  126 us
    all_to_all x1, waiting for transfers between devices, body(): lax.all_to_all(first, 'seq', split_axis=1, concat_axis=0, tiled=True)  124 us
    all_to_all x1, waiting for transfers between devices, body(): lax.all_to_all(third, 'seq', split_axis=0, concat_axis=1, tiled=True)  120 us
    unnamed x7, local copies, waits for them, and re-layouts  83 us
    all_to_all x1, starting transfers between devices, body(): lax.all_to_all(third, 'seq', split_axis=0, concat_axis=1, tiled=True)  37.2 us
    all_to_all x1, starting transfers between devices, body(): lax.all_to_all(grad_first, 'seq', split_axis=0, concat_axis=1, tiled=True)  36.5 us
  transfers between devices with their start and end apart: 7, of which 5 were waited for; matrix products, arithmetic and copies ran while one was open for 21% of the time, Pallas kernels for 0%

commit v1 on v0

--- a/solution.py
+++ b/solution.py
@@ -35,7 +35,10 @@
     grad_third = jnp.einsum(
         "fch,fhd->fcd", block_one, grad_fourth, preferred_element_type=jnp.float32
     ).astype(jnp.bfloat16)
-    arrived = lax.all_to_all(grad_third, "seq", split_axis=1, concat_axis=0, tiled=True)
+    arrived = jnp.concatenate(
+        lax.all_to_all(jnp.stack(jnp.split(grad_third, lax.axis_size("seq"), axis=1)), "seq", 0, 0),
+        axis=0,
+    )
     grad_third_cols = arrived
     grad_filtered = jnp.einsum(
         "cef,fcd->ecd", block_two, arrived, preferred_element_type=jnp.float32

time: 1200 us -> 1140 us (0.950)
  waiting for transfers between devices: 647 us -> 572 us
  matrix products: 212 us -> 225 us
    all_to_all x1, waiting for transfers between devices: 124 us -> 82.8 us  [body(): lax.all_to_all(first, 'seq', split_axis=1, concat_axis=0, tiled=True)]
    all_to_all x1, waiting for transfers between devices: 126 us -> 91.6 us  [body(): lax.all_to_all(jnp.stack(jnp.split(grad_third, lax.axis_size('seq'), axis...]
    all_to_all x1, starting transfers between devices: 7.62 us -> 36.5 us  [body(): lax.all_to_all(jnp.stack(jnp.split(grad_third, lax.axis_size('seq'), axis...]
    all_to_all x1, starting transfers between devices: 36.5 us -> 7.71 us  [body(): lax.all_to_all(first, 'seq', split_axis=1, concat_axis=0, tiled=True)]
    unnamed x7 -> x22, local copies, waits for them, and re-layouts: 83 us -> 111 us
    all_to_all x1, waiting for transfers between devices: 120 us -> 142 us  [body(): lax.all_to_all(third, 'seq', split_axis=0, concat_axis=1, tiled=True)]
    all_to_all x1, waiting for transfers between devices: 142 us -> 121 us  [body(): lax.all_to_all(grad_first, 'seq', split_axis=0, concat_axis=1, tiled=True)]
    convert_element_type x1 -> x0, local copies, waits for them, and re-layouts: 14.9 us -> none  [body(): grad_third = jnp.einsum('fch,fhd->fcd', block_one, grad_fourth, preferred...]
  transfers between devices with their start and end apart: 7 -> 7, of which waited for: 5 -> 5; matrix products, arithmetic and copies ran while one was open for 21% -> 29% of each run, Pallas kernels for 0% -> 0%
where the time goes in v1:
time: 1140 us; the launch traced here: 1130 us
  waiting for transfers between devices  572 us (50%)
  matrix products  225 us (20%)
  local copies, waits for them, and re-layouts  183 us (16%)
  starting transfers between devices  118 us (10%)
  other arithmetic  16.2 us (1%)
  between operations  14.2 us (1%)
    all_to_all x1, waiting for transfers between devices, body(): lax.all_to_all(third, 'seq', split_axis=0, concat_axis=1, tiled=True)  142 us
    reduce_scatter x1, waiting for transfers between devices, body(): lax.psum_scatter(grad_block_one, 'dp', scatter_dimension=2, tiled=True)  134 us
    all_to_all x1, waiting for transfers between devices, body(): lax.all_to_all(grad_first, 'seq', split_axis=0, concat_axis=1, tiled=True)  121 us
    unnamed x22, local copies, waits for them, and re-layouts  111 us
    all_to_all x1, waiting for transfers between devices, body(): lax.all_to_all(jnp.stack(jnp.split(grad_third, lax.axis_size('seq'), axis...  91.6 us
    all_to_all x1, waiting for transfers between devices, body(): lax.all_to_all(first, 'seq', split_axis=1, concat_axis=0, tiled=True)  82.8 us
    all_to_all x1, starting transfers between devices, body(): lax.all_to_all(grad_first, 'seq', split_axis=0, concat_axis=1, tiled=True)  37.2 us
    all_to_all x1, starting transfers between devices, body(): lax.all_to_all(third, 'seq', split_axis=0, concat_axis=1, tiled=True)  36.5 us
  transfers between devices with their start and end apart: 7, of which 5 were waited for; matrix products, arithmetic and copies ran while one was open for 29% of the time, Pallas kernels for 0%

profile of v1, /device:TPU:0, one launch (start us, length us, event | category | flops | bytes accessed | tf_op | source)
XLA Modules:
  0.0 1128.6 jit_solution(11655630146661990161)
XLA Ops:
  7.2 13.7 %fusion.21 = bf16[16,512,512]{2,1,0:T(8,128)(2,1)} fusion(bf16[16,512,512]{2,1,0:T(8,128)(2,1)} %param.10, bf16[1,16,512,512]{3,2,1,0:T(8,128)(2,1)} %param.6), kind=kOutput, calls=%fused_computation.35 | convolution fusion | flops 4299161600 | bytes 25165824 | tf_op jit(solution)/shard_map/acb,abd->acd/dot_general | solution.py:11
  20.9 11.5 %copy.77 = bf16[16,512,512]{2,0,1:T(8,128)(2,1)} copy(bf16[16,512,512]{2,1,0:T(8,128)(2,1)} %fusion.21) | data formatting | bytes 16777216 | tf_op jit(solution)/shard_map/convert_element_type | solution.py:13
  32.4 7.7 all-to-all-start
  40.1 12.3 %copy.75 = bf16[1,16,512,512]{2,3,1,0:T(8,128)(2,1)} copy(bf16[1,16,512,512]{3,2,1,0:T(8,128)(2,1)} %param.7) | data formatting | bytes 16777216 | tf_op args[1]
  52.4 12.3 %copy.84 = bf16[1,16,512,512]{2,3,1,0:T(8,128)(2,1)} copy(bf16[1,16,512,512]{3,2,1,0:T(8,128)(2,1)} %param.9) | data formatting | bytes 16777216 | tf_op args[3]
  64.6 12.9 %convert_bitcast_fusion.2 = bf16[16,512,512]{2,1,0:T(8,128)(2,1)} fusion(bf16[16,512,512]{2,1,0:T(8,128)(2,1)} %param.10, bf16[1,16,512,512]{2,3,1,0:T(8,128)(2,1)} %copy.84, bf16[1,16,512,512]{2,3,1,0:T(8,128)(2,1)} %copy.75), kind=kOutput, calls=%fused_computation.25 | convolution fusion | flops 4328521728 | bytes 33554432 | tf_op jit(solution)/shard_map/fch,fhd->fcd/dot_general | solution.py:35
  77.5 1.9 fusion.41
  79.4 1.9 fusion.40
  81.3 1.9 fusion.39
  83.3 1.9 fusion.38
  85.2 1.9 fusion.37
  88.9 1.9 fusion.35
  92.7 1.9 fusion.33
  94.6 1.9 fusion.32
  96.5 1.9 fusion.31
  100.3 1.9 fusion.29
  106.0 1.9 fusion.26
  107.9 82.8 %all-to-all-done = bf16[16,512,512]{2,0,1:T(8,128)(2,1)} async-done(((bf16[16,512,512]{2,0,1:T(8,128)(2,1)}), bf16[16,512,512]{2,0,1:T(8,128)(2,1)}, u32[]{:S(2)}, u32[]{:S(2)}) %all-to-all-start) | async-done | bytes 8388640 | tf_op jit(solution)/shard_map/all_to_all | solution.py:14
  190.6 36.5 %all-to-all-start.2 = ((bf16[16,16,32,512]{3,2,1,0:T(8,128)(2,1)}), bf16[16,16,32,512]{3,2,1,0:T(8,128)(2,1)}, u32[]{:S(2)}, u32[]{:S(2)}) async-start(bf16[16,16,32,512]{3,2,1,0:T(8,128)(2,1)} %fusion.26), calls=%async_computation.2 | async-start | bytes 16777216 | tf_op jit(solution)/shard_map/all_to_all | solution.py:39
  227.2 13.7 %copy.76 = bf16[256,32,512]{0,2,1:T(8,128)(2,1)} copy(bf16[256,32,512]{2,1,0:T(8,128)(2,1)} %param.8) | data formatting | bytes 16777216 | tf_op args[2]
  240.9 12.3 %copy.79 = bf16[16,16,32,512]{3,2,1,0:T(8,128)(2,1)} copy(bf16[16,16,32,512]{3,1,2,0:T(8,128)(2,1)} %bitcast.4) | data formatting | bytes 16777216 | tf_op jit(solution)/shard_map/all_to_all | solution.py:14
  253.2 32.9 %fusion.13 = f32[32,512,256]{2,1,0:T(8,128)} fusion(bf16[32,256,256]{2,1,0:T(8,128)(2,1)} %param.11, bf16[256,32,512]{2,1,0:T(8,128)(2,1)} %bitcast.148), kind=kOutput, calls=%fused_computation.27 | convolution fusion | flops 2147483648 | bytes 29360128 | tf_op jit(solution)/shard_map/cea,acd->ecd/dot_general | solution.py:16
  286.1 91.6 %all-to-all-done.2 = bf16[16,16,32,512]{3,2,1,0:T(8,128)(2,1)} async-done(((bf16[16,16,32,512]{3,2,1,0:T(8,128)(2,1)}), bf16[16,16,32,512]{3,2,1,0:T(8,128)(2,1)}, u32[]{:S(2)}, u32[]{:S(2)}) %all-to-all-start.2) | async-done | bytes 8388640 | tf_op jit(solution)/shard_map/all_to_all | solution.py:39
  377.8 21.9 %bitcast_multiply_fusion = (f32[256,32,512]{0,2,1:T(8,128)}, f32[32,512,256]{2,1,0:T(8,128)}) fusion(f32[32,512,256]{2,1,0:T(8,128)} %fusion.13, bf16[32,256,256]{2,1,0:T(8,128)(2,1)} %param.11, bf16[256,32,512]{2,1,0:T(8,128)(2,1)} %bitcast.31), kind=kOutput, calls=%fused_computation.10 | convolution fusion | flops 2151677952 | bytes 62914560 | tf_op jit(solution)/shard_map/cef,fcd->ecd/dot_general | solution.py:43
  399.7 21.3 %fusion.15 = f32[32,256,256]{2,1,0:T(8,128)} fusion(bf16[256,32,512]{2,1,0:T(8,128)(2,1)} %bitcast.149, bf16[256,32,512]{0,2,1:T(8,128)(2,1)} %copy.76, f32[32,512,256]{2,1,0:T(8,128)} %get-tuple-element.33), kind=kOutput, calls=%fused_computation.29 | convolution fusion | flops 2160066560 | bytes 41943040 | tf_op jit(solution)/shard_map/ecd,acd->cea/dot_general | solution.py:53
  421.0 23.1 %add_multiply_fusion.1 = f32[32,256,256]{2,1,0:T(8,128)} fusion(f32[32,256,256]{2,1,0:T(8,128)} %fusion.15, bf16[256,32,512]{2,1,0:T(8,128)(2,1)} %bitcast.31, bf16[256,32,512]{0,2,1:T(8,128)(2,1)} %copy.76, f32[32,512,256]{2,1,0:T(8,128)} %fusion.13), kind=kOutput, calls=%fused_computation.22 | convolution fusion | flops 2164260864 | bytes 50331648 | tf_op jit(solution)/shard_map/fcd,ecd->cef/dot_general | solution.py:46
  444.1 14.2 %convert_bitcast_fusion.1 = bf16[256,32,512]{0,2,1:T(8,128)(2,1)} fusion(bf16[32,256,256]{2,1,0:T(8,128)(2,1)} %param.11, bf16[256,32,512]{0,2,1:T(8,128)(2,1)} %copy.76, f32[32,512,256]{2,1,0:T(8,128)} %get-tuple-element.33), kind=kOutput, calls=%fused_computation.24 | convolution fusion | flops 2164260864 | bytes 37748736 | tf_op jit(solution)/shard_map/cea,ecd->acd/dot_general | solution.py:55
  458.3 14.8 %copy.87 = bf16[256,32,512]{2,1,0:T(8,128)(2,1)} copy(bf16[256,32,512]{0,2,1:T(8,128)(2,1)} %convert_bitcast_fusion.1) | data formatting | bytes 16777216 | tf_op jit(solution)/shard_map/convert_element_type | solution.py:57
  473.1 37.2 %all-to-all-start.3 = ((bf16[256,32,512]{2,1,0:T(8,128)(2,1)}), bf16[256,32,512]{2,1,0:T(8,128)(2,1)}, u32[]{:S(2)}, u32[]{:S(2)}) async-start(bf16[256,32,512]{2,1,0:T(8,128)(2,1)} %copy.87), calls=%async_computation.3 | async-start | bytes 16777216 | tf_op jit(solution)/shard_map/all_to_all | solution.py:58
  511.2 14.6 %convert_bitcast_fusion.3 = bf16[256,32,512]{0,2,1:T(8,128)(2,1)} fusion(bf16[32,256,256]{2,1,0:T(8,128)(2,1)} %param.11, bf16[256,32,512]{0,2,1:T(8,128)(2,1)} %copy.76, f32[32,512,256]{2,1,0:T(8,128)} %fusion.13), kind=kOutput, calls=%fused_computation.26 | convolution fusion | flops 2164260864 | bytes 37748736 | tf_op jit(solution)/shard_map/cef,ecd->fcd/dot_general | solution.py:18
  525.7 14.6 %copy.81 = bf16[256,32,512]{2,1,0:T(8,128)(2,1)} copy(bf16[256,32,512]{0,2,1:T(8,128)(2,1)} %convert_bitcast_fusion.3) | data formatting | bytes 16777216 | tf_op jit(solution)/shard_map/convert_element_type | solution.py:20
  540.4 120.6 %all-to-all-done.3 = bf16[256,32,512]{2,1,0:T(8,128)(2,1)} async-done(((bf16[256,32,512]{2,1,0:T(8,128)(2,1)}), bf16[256,32,512]{2,1,0:T(8,128)(2,1)}, u32[]{:S(2)}, u32[]{:S(2)}) %all-to-all-start.3) | async-done | bytes 8388640 | tf_op jit(solution)/shard_map/all_to_all | solution.py:58
  661.0 36.5 %all-to-all-start.1 = ((bf16[256,32,512]{2,1,0:T(8,128)(2,1)}), bf16[256,32,512]{2,1,0:T(8,128)(2,1)}, u32[]{:S(2)}, u32[]{:S(2)}) async-start(bf16[256,32,512]{2,1,0:T(8,128)(2,1)} %copy.81), calls=%async_computation.1 | async-start | bytes 16777216 | tf_op jit(solution)/shard_map/all_to_all | solution.py:21
  697.6 8.5 copy.88
  706.1 142.0 %all-to-all-done.1 = bf16[256,32,512]{2,1,0:T(8,128)(2,1)} async-done(((bf16[256,32,512]{2,1,0:T(8,128)(2,1)}), bf16[256,32,512]{2,1,0:T(8,128)(2,1)}, u32[]{:S(2)}, u32[]{:S(2)}) %all-to-all-start.1) | async-done | bytes 8388640 | tf_op jit(solution)/shard_map/all_to_all | solution.py:21
  848.1 8.2 copy.82
  856.4 16.1 %fusion.9 = f32[16,512,512]{2,1,0:T(8,128)} fusion(bf16[16,512,512]{2,1,0:T(8,128)(2,1)} %bitcast.150, bf16[1,16,512,512]{3,2,1,0:T(8,128)(2,1)} %param.6), kind=kOutput, calls=%fused_computation.18 | convolution fusion | flops 4294967296 | bytes 33554432 | tf_op jit(solution)/shard_map/acd,abd->acb/dot_general | solution.py:63
  872.4 22.1 %add_multiply_fusion = f32[16,512,512]{2,1,0:T(8,128)} fusion(f32[16,512,512]{2,1,0:T(8,128)} %fusion.9, bf16[16,512,512]{2,1,0:T(8,128)(2,1)} %bitcast.152, bf16[1,16,512,512]{2,3,1,0:T(8,128)(2,1)} %copy.84, bf16[1,16,512,512]{2,3,1,0:T(8,128)(2,1)} %copy.75), kind=kOutput, calls=%fused_computation.14 | convolution fusion | flops 4332716032 | bytes 58720256 | tf_op jit(solution)/shard_map/fhd,fcd->fch/dot_general | solution.py:32
  894.5 11.4 %convert_bitcast_fusion = bf16[1,16,512,512]{2,3,1,0:T(8,128)(2,1)} fusion(bf16[16,512,512]{2,1,0:T(8,128)(2,1)} %bitcast.151, bf16[16,512,512]{2,1,0:T(8,128)(2,1)} %param.10), kind=kOutput, calls=%fused_computation.23 | convolution fusion | flops 4299161600 | bytes 25165824 | tf_op jit(solution)/shard_map/acb,acd->abd/dot_general | solution.py:59
  905.9 12.3 %copy.96 = bf16[1,16,512,512]{3,2,1,0:T(8,128)(2,1)} copy(bf16[1,16,512,512]{2,3,1,0:T(8,128)(2,1)} %convert_bitcast_fusion) | data formatting | bytes 16777216
  918.2 20.7 %fusion.8 = (bf16[1,16,512,512]{2,3,1,0:T(8,128)(2,1)}, bf16[1,16,512,512]{2,3,1,0:T(8,128)(2,1)}) fusion(bf16[1,16,512,512]{2,3,1,0:T(8,128)(2,1)} %copy.84, bf16[1,16,512,512]{2,3,1,0:T(8,128)(2,1)} %copy.75, bf16[16,512,512]{2,1,0:T(8,128)(2,1)} %bitcast.153, bf16[16,512,512]{2,1,0:T(8,128)(2,1)} %param.10), kind=kOutput, calls=%fused_computation.17 | convolution fusion | flops 4353687552 | bytes 50331648 | tf_op jit(solution)/shard_map/fch,fcd->fhd/dot_general | solution.py:23
  938.8 12.3 %copy.95 = bf16[1,16,512,512]{3,2,1,0:T(8,128)(2,1)} copy(bf16[1,16,512,512]{2,3,1,0:T(8,128)(2,1)} %get-tuple-element.31) | data formatting | bytes 16777216
  951.2 12.3 %copy.97 = bf16[1,16,512,512]{3,2,1,0:T(8,128)(2,1)} copy(bf16[1,16,512,512]{2,3,1,0:T(8,128)(2,1)} %get-tuple-element.30) | data formatting | bytes 16777216
  963.5 4.1 convert_element_type.97
  967.6 6.2 convert_element_type.95
  973.8 7.8 copy.98
  981.6 134.1 %reduce-scatter.6.cloned.1.call-done = f32[16,512,256]{2,1,0:T(8,128)} async-done(((f32[16,512,512]{2,1,0:T(8,128)}), f32[16,512,256]{2,1,0:T(8,128)}) %reduce-scatter.6.cloned.1.call-update) | async-done | bytes 8388624 | tf_op jit(solution)/shard_map/reduce_scatter | solution.py:66
  1115.7 5.9 convert_element_type.96
  (13 shorter events, 10.2 us)
Async XLA Ops:
  32.4 158.3 %all-to-all-start = ((bf16[16,512,512]{2,0,1:T(8,128)(2,1)}), bf16[16,512,512]{2,0,1:T(8,128)(2,1)}, u32[]{:S(2)}, u32[]{:S(2)}) async-start(bf16[16,512,512]{2,0,1:T(8,128)(2,1)} %copy.77), calls=%async_computation | async-start | bytes 16777216 | tf_op jit(solution)/shard_map/all_to_all | solution.py:14
  190.6 187.1 %all-to-all-start.2 = ((bf16[16,16,32,512]{3,2,1,0:T(8,128)(2,1)}), bf16[16,16,32,512]{3,2,1,0:T(8,128)(2,1)}, u32[]{:S(2)}, u32[]{:S(2)}) async-start(bf16[16,16,32,512]{3,2,1,0:T(8,128)(2,1)} %fusion.26), calls=%async_computation.2 | async-start | bytes 16777216 | tf_op jit(solution)/shard_map/all_to_all | solution.py:39
  227.2 736.3 %reduce-scatter.8.cloned.1.call-start = ((), (), s32[]{:S(2)}) async-start(), calls=%async_computation.9 | async-start | bytes 12582912 | tf_op jit(solution)/shard_map/reduce_scatter | solution.py:67
  473.1 187.8 %all-to-all-start.3 = ((bf16[256,32,512]{2,1,0:T(8,128)(2,1)}), bf16[256,32,512]{2,1,0:T(8,128)(2,1)}, u32[]{:S(2)}, u32[]{:S(2)}) async-start(bf16[256,32,512]{2,1,0:T(8,128)(2,1)} %copy.87), calls=%async_computation.3 | async-start | bytes 16777216 | tf_op jit(solution)/shard_map/all_to_all | solution.py:58
  510.4 457.2 %reduce-scatter.4.cloned.1.call-start = ((), (), s32[]{:S(2)}) async-start(), calls=%async_computation.7 | async-start | bytes 25165824 | tf_op jit(solution)/shard_map/reduce_scatter | solution.py:68
  661.0 187.1 %all-to-all-start.1 = ((bf16[256,32,512]{2,1,0:T(8,128)(2,1)}), bf16[256,32,512]{2,1,0:T(8,128)(2,1)}, u32[]{:S(2)}, u32[]{:S(2)}) async-start(bf16[256,32,512]{2,1,0:T(8,128)(2,1)} %copy.81), calls=%async_computation.1 | async-start | bytes 16777216 | tf_op jit(solution)/shard_map/all_to_all | solution.py:21
  697.5 418.2 %reduce-scatter.6.cloned.1.call-start = ((), (), s32[]{:S(2)}) async-start(), calls=%async_computation.8 | async-start | bytes 25165824 | tf_op jit(solution)/shard_map/reduce_scatter | solution.py:66
Sparse Core Ops, SparseCore 0:
  444.2 131.1 reduce-scatter.7
  577.7 189.1 reduce-scatter.3
  894.6 220.9 reduce-scatter.5
